TPU v7x, 512 devices: a whole 4x8x8 slice. The times are simulated.
512 devices in a mesh: shift: 4 (over x_hi, core), space: 128 (over y, z, x_lo).
Axes of the slice: x: 4 (x_hi: 2, x_lo: 2; x = x_hi * 2 + x_lo), y: 8, z: 8, core: 2. Of those that a mesh axis runs over, the one named last changes fastest.
Arguments:
- labels: int32 [256, 32, 256], P('space'), may hold values from 0 to 7
- conductance: float32 [8], replicated, may hold values from 0.2 to 5
- capacity_table: float32 [8], replicated, may hold values from 0.5 to 2
- shift_values: float32 [8], replicated, may hold values from 0.1 to 4
- prior_basis: float32 [256, 256, 32, 256], P(None, 'space', 'shift'), may hold values from -6 to 6
Outputs:
- new_block: float32 [8, 8, 256, 32, 256], P(None, None, 'space', 'shift')
- coefficients: float32 [64, 256], replicated
- factor: float32 [64, 64], replicated
All inputs are finite; a program needn't handle non-finite values.
Results may differ from a plain program's by a relative error of at most 0.0003.
Values sent between devices are 32-bit elements; how exact they have to be, the bound alone decides.
No kernel may reach another device: no remote copies, remote signals or barrier semaphores. Data moves between devices by JAX's collectives and lax.ppermute only.
A program may use at most 64 MiB of HBM per device.

v0:
```python
import jax
import jax.numpy as jnp
from jax import lax
from jax.sharding import PartitionSpec as P

COLS = 8
SWEEPS = 4
LOWER_BOUND = 0.1
UPPER_BOUND = 2.0


def padded_2(cells, sides, width):
    for axis, dim in sides:
        count = lax.axis_size(axis)
        ends = count - 1
        head = lax.slice_in_dim(cells, 0, width, axis=dim)
        tail = lax.slice_in_dim(cells, cells.shape[dim] - width, cells.shape[dim], axis=dim)
        cells = jnp.concatenate(
            [
                lax.ppermute(tail, axis, [(i, (i + 1) % count) for i in range(ends)]),
                cells,
                lax.ppermute(head, axis, [((i + 1) % count, i) for i in range(ends)]),
            ],
            axis=dim,
        )
    return cells


def lookup(labels, table):
    materials = jnp.arange(table.shape[0], dtype=jnp.int32)
    onehot = (labels[None] == materials[:, None, None, None]).astype(jnp.float32)
    return jnp.sum(onehot * table[:, None, None, None], axis=0)


def conductances(conduct, padded):
    west_face = 0.5 * (conduct + padded[:-2, 1:-1, 1:-1])
    east_face = 0.5 * (conduct + padded[2:, 1:-1, 1:-1])
    south_face = 0.5 * (conduct + padded[1:-1, :-2, 1:-1])
    north_face = 0.5 * (conduct + padded[1:-1, 2:, 1:-1])
    below_face = 0.5 * (conduct + padded[1:-1, 1:-1, :-2])
    above_face = 0.5 * (conduct + padded[1:-1, 1:-1, 2:])
    return (west_face, east_face, south_face, north_face, below_face, above_face)


def neighbours(padded, face_list):
    west_face, east_face, south_face, north_face, below_face, above_face = face_list
    summed = west_face * padded[..., :-2, 1:-1, 1:-1] + east_face * padded[..., 2:, 1:-1, 1:-1]
    summed = (
        summed
        + south_face * padded[..., 1:-1, :-2, 1:-1]
        + north_face * padded[..., 1:-1, 2:, 1:-1]
    )
    summed = (
        summed
        + below_face * padded[..., 1:-1, 1:-1, :-2]
        + above_face * padded[..., 1:-1, 1:-1, 2:]
    )
    return summed


def diagonal_of(face_list, shift_list, capacity):
    west_face, east_face, south_face, north_face, below_face, above_face = face_list
    summed = west_face + east_face + (south_face + north_face) + (below_face + above_face)
    return summed[None, None] + shift_list[:, None, None, None, None] * capacity[None, None]


def chebyshev(source, face_list, diagonal, padder):
    center = 0.5 * (UPPER_BOUND + LOWER_BOUND)
    spread = 0.5 * (UPPER_BOUND - LOWER_BOUND)
    ratio_value = center / spread
    reciprocal = 1.0 / diagonal
    solution = jnp.zeros_like(source)
    remainder = source
    weight_old = 1.0 / ratio_value
    direction = reciprocal * remainder / center
    for sweep_index in range(SWEEPS):
        solution = solution + direction
        if sweep_index + 1 < SWEEPS:
            applied = diagonal * direction - neighbours(padder(direction), face_list)
            remainder = remainder - applied
            weight_new = 1.0 / (2.0 * ratio_value - weight_old)
            direction = weight_new * weight_old * direction + 2.0 * weight_new / spread * (
                reciprocal * remainder
            )
            weight_old = weight_new
    return solution


def products(left_side, right_side):
    return lax.dot_general(
        left_side, right_side, (((1,), (1,)), ((), ())), precision=lax.Precision.HIGHEST
    )


def matmul(left_side, right_side):
    return jnp.dot(left_side, right_side, precision=lax.Precision.HIGHEST)


def local(labels, conductance, capacity_table, shift_values, prior_basis):
    groups = lax.axis_size("shift")
    shifts_all = shift_values.shape[0]
    per_device = shifts_all // groups
    new_count = shifts_all * COLS
    basis_count = prior_basis.shape[0]
    slab_x = prior_basis.shape[1]
    quarter = prior_basis.shape[2]
    depth = prior_basis.shape[3]
    flat_basis = prior_basis.reshape(basis_count, slab_x * quarter * depth)
    cell_weight = 1.0 / (slab_x * quarter * depth * groups * lax.axis_size("space"))
    tail_columns = prior_basis[basis_count - new_count :]
    conduct = lookup(labels, conductance)
    capacity = lookup(labels, capacity_table)
    rimmed = padded_2(conduct, (("space", 0),), 1)
    face_list = conductances(conduct, jnp.pad(rimmed, ((0, 0), (1, 1), (1, 1))))
    shift_list = lax.dynamic_slice_in_dim(
        shift_values, lax.axis_index("shift") * per_device, per_device, 0
    )
    diagonal = diagonal_of(face_list, shift_list, capacity)
    starting = lax.all_to_all(tail_columns, "shift", split_axis=0, concat_axis=2, tiled=True)
    full_y = starting.shape[2]
    source = starting.reshape(per_device, COLS, slab_x, full_y, depth) * capacity[None, None]

    def padder(field):
        widened = padded_2(field, (("space", 2),), 1)
        return jnp.pad(widened, ((0, 0), (0, 0), (0, 0), (1, 1), (1, 1)))

    fields = chebyshev(source, face_list, diagonal, padder)
    merged = fields.reshape(per_device * COLS, slab_x, full_y, depth)
    regrouped = lax.all_to_all(merged, "shift", split_axis=2, concat_axis=0, tiled=True)
    columns = regrouped.reshape(new_count, slab_x * quarter * depth)
    first_proj = lax.psum(products(columns, flat_basis), ("shift", "space")) * cell_weight
    columns = columns - matmul(first_proj, flat_basis)
    second_proj = lax.psum(products(columns, flat_basis), ("shift", "space")) * cell_weight
    columns = columns - matmul(second_proj, flat_basis)
    gram_matrix = lax.psum(products(columns, columns), ("shift", "space")) * cell_weight
    factor = jnp.linalg.cholesky(gram_matrix)
    orthonormal = lax.linalg.triangular_solve(factor, columns, left_side=True, lower=True)
    new_block = orthonormal.reshape(shifts_all, COLS, slab_x, quarter, depth)
    return (new_block, first_proj + second_proj, factor)


def solution(mesh):
    in_specs = (P("space", None, None), P(), P(), P(), P(None, "space", "shift", None))
    out_specs = (P(None, None, "space", "shift", None), P(), P())
    return jax.shard_map(local, mesh=mesh, in_specs=in_specs, out_specs=out_specs, check_vma=False)
```

profile of v0, /device:TPU:1, one launch (start us, length us, event | category | flops | bytes accessed | tf_op | source)
XLA Modules:
  0.0 803.1 jit_solution(15233755541338323633)
XLA Ops:
  7.2 2.3 slice.133
  9.5 10.4 %all-to-all-start = ((f32[64,2,8,256]{3,2,1,0:T(8,128)}), f32[64,2,8,256]{3,2,1,0:T(8,128)S(1)}, u32[]{:S(2)}, u32[]{:S(2)}) async-start(f32[64,2,8,256]{3,2,1,0:T(8,128)} %slice.133), calls=%async_computation | async-start | bytes 2097152 | tf_op jit(solution)/shard_map/all_to_all | solution.py:119
  21.4 1.3 collective-permute-start.1
  22.8 10.3 %collective-permute-done = f32[1,32,256]{2,1,0:T(8,128)S(1)} collective-permute-done((f32[1,32,256]{2,1,0:T(8,128)S(1)}, f32[1,32,256]{2,1,0:T(8,128)S(1)}, u32[]{:S(2)}, u32[]{:S(2)}) %collective-permute-start) | collective-permute-done | bytes 32800 | tf_op jit(solution)/shard_map/ppermute | solution.py:20
  33.4 2.3 all-to-all-done
  36.1 1.9 collective-permute-start.2
  37.9 1.3 collective-permute-start.3
  39.2 20.6 %collective-permute-done.2 = f32[2,8,1,32,256]{4,3,2,1,0:T(8,128)S(1)} collective-permute-done((f32[2,8,1,32,256]{4,3,2,1,0:T(8,128)S(1)}, f32[2,8,1,32,256]{4,3,2,1,0:T(8,128)S(1)}, u32[]{:S(2)}, u32[]{:S(2)}) %collective-permute-start.2) | collective-permute-done | bytes 524320 | tf_op jit(solution)/shard_map/ppermute | solution.py:20
  59.8 1.8 select_maximum_fusion.4
  62.9 4.1 collective-permute-start.4
  67.1 1.3 collective-permute-start.5
  68.4 19.6 %collective-permute-done.4 = f32[2,8,1,32,256]{4,3,2,1,0:T(8,128)S(1)} collective-permute-done((f32[2,8,1,32,256]{4,3,2,1,0:T(8,128)S(1)}, f32[2,8,1,32,256]{4,3,2,1,0:T(8,128)S(1)}, u32[]{:S(2)}, u32[]{:S(2)}) %collective-permute-start.4) | collective-permute-done | bytes 524320 | tf_op jit(solution)/shard_map/ppermute | solution.py:20
  88.0 1.8 select_maximum_fusion.2
  91.1 4.1 collective-permute-start.6
  95.3 1.3 collective-permute-start.7
  96.6 18.6 %collective-permute-done.6 = f32[2,8,1,32,256]{4,3,2,1,0:T(8,128)S(1)} collective-permute-done((f32[2,8,1,32,256]{4,3,2,1,0:T(8,128)S(1)}, f32[2,8,1,32,256]{4,3,2,1,0:T(8,128)S(1)}, u32[]{:S(2)}, u32[]{:S(2)}) %collective-permute-start.6) | collective-permute-done | bytes 524320 | tf_op jit(solution)/shard_map/ppermute | solution.py:20
  115.1 1.8 select_maximum_fusion
  117.0 1.4 fusion.9
  118.3 1.8 copy.36
  120.1 6.9 all-to-all-start.1
  127.0 7.9 copy.46
  135.0 7.2 all-to-all-done.1
  143.1 6.8 fusion.71
  150.2 267.6 %all-reduce.7.cloned.1.call-done = f32[64,256]{1,0:T(8,128)} async-done(((f32[64,256]{1,0:T(8,128)}), f32[64,256]{1,0:T(8,128)}) %all-reduce.7.cloned.1.call-update) | async-done | bytes 65552 | tf_op jit(solution)/shard_map/psum | solution.py:131
  417.8 5.0 convolution_subtract_fusion.1
  422.7 4.6 fusion.72
  427.4 251.4 %all-reduce.9.cloned.1.call-done = f32[64,256]{1,0:T(8,128)} async-done(((f32[64,256]{1,0:T(8,128)}), f32[64,256]{1,0:T(8,128)}) %all-reduce.9.cloned.1.call-update) | async-done | bytes 65552 | tf_op jit(solution)/shard_map/psum | solution.py:133
  678.8 4.8 convolution_subtract_fusion
  684.6 94.9 %psum.23 = f32[64,64]{0,1:T(8,128)S(1)} all-reduce(f32[64,64]{0,1:T(8,128)S(1)} %fusion.73), channel_id=1, replica_groups=mesh['shift'=4,'space'=128] {'shift','space'}, use_global_device_ids=true, to_apply=%region_4.5 | all-reduce | flops 4096 | bytes 32768 | tf_op jit(solution)/shard_map/psum | solution.py:135
  779.6 5.8 cholesky.16
  787.4 4.9 custom-call.6
  792.7 1.6 fusion.34
  (50 shorter events, 11.4 us)
Async XLA Ops:
  7.2 12.7 %copy-start.5 = (f32[8]{0:T(128)S(1)}, f32[8]{0:T(128)}, u32[]{:S(2)}) copy-start(f32[8]{0:T(128)} %param.7) | copy-start | bytes 100
  7.2 12.7 %copy-start.4 = (f32[8]{0:T(128)S(1)}, f32[8]{0:T(128)}, u32[]{:S(2)}) copy-start(f32[8]{0:T(128)} %param.6) | copy-start | bytes 100
  7.2 12.7 %copy-start.3 = (s32[2,32,256]{2,1,0:T(8,128)S(1)}, s32[2,32,256]{2,1,0:T(8,128)}, u32[]{:S(2)}) copy-start(s32[2,32,256]{2,1,0:T(8,128)} %param.5) | copy-start | bytes 196612
  7.2 15.5 %copy-start.6 = (f32[8]{0:T(128)S(1)}, f32[8]{0:T(128)}, u32[]{:S(2)}) copy-start(f32[8]{0:T(128)} %param.8) | copy-start | bytes 100
  9.5 26.2 %all-to-all-start = ((f32[64,2,8,256]{3,2,1,0:T(8,128)}), f32[64,2,8,256]{3,2,1,0:T(8,128)S(1)}, u32[]{:S(2)}, u32[]{:S(2)}) async-start(f32[64,2,8,256]{3,2,1,0:T(8,128)} %slice.133), calls=%async_computation | async-start | bytes 2097152 | tf_op jit(solution)/shard_map/all_to_all | solution.py:119
  20.1 13.0 %collective-permute-start = (f32[1,32,256]{2,1,0:T(8,128)S(1)}, f32[1,32,256]{2,1,0:T(8,128)S(1)}, u32[]{:S(2)}, u32[]{:S(2)}) collective-permute-start(f32[1,32,256]{2,1,0:T(8,128)S(1)} %get-tuple-element.42), channel_id=1, source_target_pairs={{0,1},{1,2},{2,3},{3,4},{4,5},{5,6},{6,7},{7,8},{8,9},{9,10},{10,1... | collective-permute-start | bytes 98312 | tf_op jit(solution)/shard_map/ppermute | solution.py:20
  21.4 11.7 %collective-permute-start.1 = (f32[1,32,256]{2,1,0:T(8,128)S(1)}, f32[1,32,256]{2,1,0:T(8,128)S(1)}, u32[]{:S(2)}, u32[]{:S(2)}) collective-permute-start(f32[1,32,256]{2,1,0:T(8,128)S(1)} %get-tuple-element.43), channel_id=1, source_target_pairs={{1,0},{2,1},{3,2},{4,3},{5,4},{6,5},{7,6},{8,7},{9,8},{10,9},{11,1... | collective-permute-start | bytes 98312 | tf_op jit(solution)/shard_map/ppermute | solution.py:22
  36.1 23.7 %collective-permute-start.2 = (f32[2,8,1,32,256]{4,3,2,1,0:T(8,128)S(1)}, f32[2,8,1,32,256]{4,3,2,1,0:T(8,128)S(1)}, u32[]{:S(2)}, u32[]{:S(2)}) collective-permute-start(f32[2,8,1,32,256]{4,3,2,1,0:T(8,128)S(1)} %get-tuple-element.37), channel_id=1, source_target_pairs={{0,1},{1,2},{2,3},{3,4},{4,5},{5,6},{6,7},{7,8},{8,9},{9,10},{10,1... | collective-permute-start | bytes 1572872 | tf_op jit(solution)/shard_map/ppermute | solution.py:20
  37.9 21.9 %collective-permute-start.3 = (f32[2,8,1,32,256]{4,3,2,1,0:T(8,128)S(1)}, f32[2,8,1,32,256]{4,3,2,1,0:T(8,128)S(1)}, u32[]{:S(2)}, u32[]{:S(2)}) collective-permute-start(f32[2,8,1,32,256]{4,3,2,1,0:T(8,128)S(1)} %get-tuple-element.38), channel_id=1, source_target_pairs={{1,0},{2,1},{3,2},{4,3},{5,4},{6,5},{7,6},{8,7},{9,8},{10,9},{11,1... | collective-permute-start | bytes 1572872 | tf_op jit(solution)/shard_map/ppermute | solution.py:22
  62.9 25.1 %collective-permute-start.4 = (f32[2,8,1,32,256]{4,3,2,1,0:T(8,128)S(1)}, f32[2,8,1,32,256]{4,3,2,1,0:T(8,128)S(1)}, u32[]{:S(2)}, u32[]{:S(2)}) collective-permute-start(f32[2,8,1,32,256]{4,3,2,1,0:T(8,128)S(1)} %get-tuple-element.35), channel_id=1, source_target_pairs={{0,1},{1,2},{2,3},{3,4},{4,5},{5,6},{6,7},{7,8},{8,9},{9,10},{10,1... | collective-permute-start | bytes 1572872 | tf_op jit(solution)/shard_map/ppermute | solution.py:20
  67.1 20.9 %collective-permute-start.5 = (f32[2,8,1,32,256]{4,3,2,1,0:T(8,128)S(1)}, f32[2,8,1,32,256]{4,3,2,1,0:T(8,128)S(1)}, u32[]{:S(2)}, u32[]{:S(2)}) collective-permute-start(f32[2,8,1,32,256]{4,3,2,1,0:T(8,128)S(1)} %get-tuple-element.36), channel_id=1, source_target_pairs={{1,0},{2,1},{3,2},{4,3},{5,4},{6,5},{7,6},{8,7},{9,8},{10,9},{11,1... | collective-permute-start | bytes 1572872 | tf_op jit(solution)/shard_map/ppermute | solution.py:22
  91.1 24.0 %collective-permute-start.6 = (f32[2,8,1,32,256]{4,3,2,1,0:T(8,128)S(1)}, f32[2,8,1,32,256]{4,3,2,1,0:T(8,128)S(1)}, u32[]{:S(2)}, u32[]{:S(2)}) collective-permute-start(f32[2,8,1,32,256]{4,3,2,1,0:T(8,128)S(1)} %get-tuple-element.33), channel_id=1, source_target_pairs={{0,1},{1,2},{2,3},{3,4},{4,5},{5,6},{6,7},{7,8},{8,9},{9,10},{10,1... | collective-permute-start | bytes 1572872 | tf_op jit(solution)/shard_map/ppermute | solution.py:20
  95.3 19.9 %collective-permute-start.7 = (f32[2,8,1,32,256]{4,3,2,1,0:T(8,128)S(1)}, f32[2,8,1,32,256]{4,3,2,1,0:T(8,128)S(1)}, u32[]{:S(2)}, u32[]{:S(2)}) collective-permute-start(f32[2,8,1,32,256]{4,3,2,1,0:T(8,128)S(1)} %get-tuple-element.34), channel_id=1, source_target_pairs={{1,0},{2,1},{3,2},{4,3},{5,4},{6,5},{7,6},{8,7},{9,8},{10,9},{11,1... | collective-permute-start | bytes 1572872 | tf_op jit(solution)/shard_map/ppermute | solution.py:22
  120.1 22.0 %all-to-all-start.1 = ((f32[16,2,32,256]{3,1,0,2:T(2,128)}), f32[16,2,32,256]{3,1,0,2:T(2,128)S(1)}, u32[]{:S(2)}, u32[]{:S(2)}) async-start(f32[16,2,32,256]{3,1,0,2:T(2,128)} %copy.36), calls=%async_computation.1 | async-start | bytes 2097152 | tf_op jit(solution)/shard_map/all_to_all | solution.py:129
  127.0 290.7 %all-reduce.7.cloned.1.call-start = ((), (), s32[]{:S(2)}) async-start(), calls=%async_computation.2 | async-start | bytes 131072 | tf_op jit(solution)/shard_map/psum | solution.py:131
  149.9 528.9 %all-reduce.9.cloned.1.call-start = ((), (), s32[]{:S(2)}) async-start(), calls=%async_computation.3 | async-start | bytes 131072 | tf_op jit(solution)/shard_map/psum | solution.py:133
  417.8 5.0 copy-start
  684.6 111.0 %copy-start.1 = (f32[64,256]{1,0:T(8,128)S(1)}, f32[64,256]{1,0:T(8,128)}, u32[]{:S(2)}) copy-start(f32[64,256]{1,0:T(8,128)} %all-reduce.7.cloned.1.call-done) | copy-start | bytes 196612
  684.6 111.0 %copy-start.2 = (f32[64,256]{1,0:T(8,128)S(1)}, f32[64,256]{1,0:T(8,128)}, u32[]{:S(2)}) copy-start(f32[64,256]{1,0:T(8,128)} %all-reduce.9.cloned.1.call-done) | copy-start | bytes 196612
Sparse Core Ops, SparseCore 0:
  150.0 267.6 all-reduce.6
  427.5 251.2 all-reduce.8
where the time goes:
time: 804 us; the launch traced here: 803 us
  waiting for transfers between devices  598 us (74%)
  blocking collectives  94.9 us (12%)
  starting transfers between devices  34.2 us (4%)
  matrix products  23.7 us (3%)
  other arithmetic  23.2 us (3%)
  local copies, waits for them, and re-layouts  15.2 us (2%)
  between operations  14.3 us (2%)
    psum x2, waiting for transfers between devices, local(): lax.psum(products(columns, flat_basis), ('shift', 'space')) * cell_weight  519 us
    psum x1, blocking collectives, local(): lax.psum(products(columns, columns), ('shift', 'space')) * cell_weight  94.9 us
    ppermute x4, waiting for transfers between devices, padded_2(): lax.ppermute(tail, axis, [(i, (i + 1) % count) for i in range(ends)])  69 us
  transfers between devices with their start and end apart: 12, of which 8 were waited for; matrix products, arithmetic and copies ran while one was open for 1% of the time, Pallas kernels for 0%

commit v1 on v0

--- a/solution.py
+++ b/solution.py
@@ -97,6 +97,10 @@
 
 
 def local(labels, conductance, capacity_table, shift_values, prior_basis):
+
+    def show_columns(point):
+        return lax.all_gather(point, ("shift", "space")).sum(axis=0)
+
     groups = lax.axis_size("shift")
     shifts_all = shift_values.shape[0]
     per_device = shifts_all // groups
@@ -128,7 +132,7 @@
     merged = fields.reshape(per_device * COLS, slab_x, full_y, depth)
     regrouped = lax.all_to_all(merged, "shift", split_axis=2, concat_axis=0, tiled=True)
     columns = regrouped.reshape(new_count, slab_x * quarter * depth)
-    first_proj = lax.psum(products(columns, flat_basis), ("shift", "space")) * cell_weight
+    first_proj = show_columns(products(columns, flat_basis)) * cell_weight
     columns = columns - matmul(first_proj, flat_basis)
     second_proj = lax.psum(products(columns, flat_basis), ("shift", "space")) * cell_weight
     columns = columns - matmul(second_proj, flat_basis)

time: 804 us -> 2030 us (2.52)
  waiting for transfers between devices: 598 us -> 1810 us
    all_gather x0 -> x1, waiting for transfers between devices: none -> 1470 us  [show_columns(): return lax.all_gather(point, ('shift', 'space')).sum(axis=0)]
    psum x2 -> x1, waiting for transfers between devices: 519 us -> 262 us  [local(): lax.psum(products(columns, flat_basis), ('shift', 'space')) * cell_weight]
  transfers between devices with their start and end apart: 12 -> 12, of which waited for: 8 -> 8; matrix products, arithmetic and copies ran while one was open for 1% -> 0% of each run, Pallas kernels for 0% -> 0%
where the time goes in v1:
time: 2030 us
  waiting for transfers between devices  1810 us (89%)
  blocking collectives  94.9 us (5%)
  other arithmetic  36.1 us (2%)
  starting transfers between devices  34.2 us (2%)
  matrix products  23.7 us (1%)
    all_gather x1, waiting for transfers between devices, show_columns(): return lax.all_gather(point, ('shift', 'space')).sum(axis=0)  1470 us
    psum x1, waiting for transfers between devices, local(): lax.psum(products(columns, flat_basis), ('shift', 'space')) * cell_weight  262 us
    psum x1, blocking collectives, local(): lax.psum(products(columns, columns), ('shift', 'space')) * cell_weight  94.9 us
    ppermute x4, waiting for transfers between devices, padded_2(): lax.ppermute(tail, axis, [(i, (i + 1) % count) for i in range(ends)])  69 us
  transfers between devices with their start and end apart: 12, of which 8 were waited for; matrix products, arithmetic and copies ran while one was open for 0% of the time, Pallas kernels for 0%

profile of v1, /device:TPU:1, one launch (start us, length us, event | category | flops | bytes accessed | tf_op | source)
XLA Modules:
  0.0 2027.0 jit_solution(7498677983524243202)
XLA Ops:
  7.2 2.3 slice.133
  9.5 10.4 all-to-all-start
  21.4 1.3 collective-permute-start.1
  22.8 10.3 collective-permute-done
  33.4 2.3 all-to-all-done
  36.1 1.9 collective-permute-start.2
  37.9 1.3 collective-permute-start.3
  39.2 20.6 %collective-permute-done.2 = f32[2,8,1,32,256]{4,3,2,1,0:T(8,128)S(1)} collective-permute-done((f32[2,8,1,32,256]{4,3,2,1,0:T(8,128)S(1)}, f32[2,8,1,32,256]{4,3,2,1,0:T(8,128)S(1)}, u32[]{:S(2)}, u32[]{:S(2)}) %collective-permute-start.2) | collective-permute-done | bytes 524320 | tf_op jit(solution)/shard_map/ppermute | solution.py:20
  59.8 1.8 select_maximum_fusion.4
  62.9 4.1 collective-permute-start.4
  67.1 1.3 collective-permute-start.5
  68.4 19.6 collective-permute-done.4
  88.0 1.8 select_maximum_fusion.2
  91.1 4.1 collective-permute-start.6
  96.5 18.6 collective-permute-done.6
  115.1 1.8 select_maximum_fusion
  116.9 1.4 fusion.9
  118.3 1.8 copy.36
  120.1 6.9 all-to-all-start.1
  127.0 8.0 copy.46
  135.1 7.1 all-to-all-done.1
  143.1 6.8 fusion.71
  150.2 1468.3 %all-gather.3.cloned.1.call-done = f32[32768,256]{1,0:T(8,128)} async-done(((f32[64,256]{1,0:T(8,128)}), f32[32768,256]{1,0:T(8,128)}) %all-gather.3.cloned.1.call-update) | async-done | bytes 33554448 | tf_op jit(solution)/shard_map/all_gather | solution.py:102
  1618.4 12.9 reduce_sum.29
  1631.4 5.0 convolution_subtract_fusion.1
  1636.3 4.6 fusion.72
  1641.0 261.8 %all-reduce.6.cloned.1.call-done = f32[64,256]{1,0:T(8,128)} async-done(((f32[64,256]{1,0:T(8,128)}), f32[64,256]{1,0:T(8,128)}) %all-reduce.6.cloned.1.call-update) | async-done | bytes 65552 | tf_op jit(solution)/shard_map/psum | solution.py:137
  1902.7 4.8 convolution_subtract_fusion
  1908.6 94.9 %psum.15 = f32[64,64]{0,1:T(8,128)S(1)} all-reduce(f32[64,64]{0,1:T(8,128)S(1)} %fusion.73), channel_id=1, replica_groups=mesh['shift'=4,'space'=128] {'shift','space'}, use_global_device_ids=true, to_apply=%region_4.5 | all-reduce | flops 4096 | bytes 32768 | tf_op jit(solution)/shard_map/psum | solution.py:139
  2003.6 5.8 cholesky.16
  2011.3 4.9 custom-call.6
  2016.7 1.6 fusion.34
  (49 shorter events, 12.7 us)
Async XLA Ops:
  7.2 12.7 copy-start.4
  7.2 12.7 copy-start.3
  7.2 12.7 copy-start.2
  7.2 15.5 copy-start.5
  9.5 26.2 %all-to-all-start = ((f32[64,2,8,256]{3,2,1,0:T(8,128)}), f32[64,2,8,256]{3,2,1,0:T(8,128)S(1)}, u32[]{:S(2)}, u32[]{:S(2)}) async-start(f32[64,2,8,256]{3,2,1,0:T(8,128)} %slice.133), calls=%async_computation | async-start | bytes 2097152 | tf_op jit(solution)/shard_map/all_to_all | solution.py:123
  20.1 13.0 collective-permute-start
  21.4 11.7 collective-permute-start.1
  36.1 23.7 %collective-permute-start.2 = (f32[2,8,1,32,256]{4,3,2,1,0:T(8,128)S(1)}, f32[2,8,1,32,256]{4,3,2,1,0:T(8,128)S(1)}, u32[]{:S(2)}, u32[]{:S(2)}) collective-permute-start(f32[2,8,1,32,256]{4,3,2,1,0:T(8,128)S(1)} %get-tuple-element.37), channel_id=1, source_target_pairs={{0,1},{1,2},{2,3},{3,4},{4,5},{5,6},{6,7},{7,8},{8,9},{9,10},{10,1... | collective-permute-start | bytes 1572872 | tf_op jit(solution)/shard_map/ppermute | solution.py:20
  37.9 21.9 %collective-permute-start.3 = (f32[2,8,1,32,256]{4,3,2,1,0:T(8,128)S(1)}, f32[2,8,1,32,256]{4,3,2,1,0:T(8,128)S(1)}, u32[]{:S(2)}, u32[]{:S(2)}) collective-permute-start(f32[2,8,1,32,256]{4,3,2,1,0:T(8,128)S(1)} %get-tuple-element.38), channel_id=1, source_target_pairs={{1,0},{2,1},{3,2},{4,3},{5,4},{6,5},{7,6},{8,7},{9,8},{10,9},{11,1... | collective-permute-start | bytes 1572872 | tf_op jit(solution)/shard_map/ppermute | solution.py:22
  62.9 25.1 %collective-permute-start.4 = (f32[2,8,1,32,256]{4,3,2,1,0:T(8,128)S(1)}, f32[2,8,1,32,256]{4,3,2,1,0:T(8,128)S(1)}, u32[]{:S(2)}, u32[]{:S(2)}) collective-permute-start(f32[2,8,1,32,256]{4,3,2,1,0:T(8,128)S(1)} %get-tuple-element.35), channel_id=1, source_target_pairs={{0,1},{1,2},{2,3},{3,4},{4,5},{5,6},{6,7},{7,8},{8,9},{9,10},{10,1... | collective-permute-start | bytes 1572872 | tf_op jit(solution)/shard_map/ppermute | solution.py:20
  67.1 20.9 %collective-permute-start.5 = (f32[2,8,1,32,256]{4,3,2,1,0:T(8,128)S(1)}, f32[2,8,1,32,256]{4,3,2,1,0:T(8,128)S(1)}, u32[]{:S(2)}, u32[]{:S(2)}) collective-permute-start(f32[2,8,1,32,256]{4,3,2,1,0:T(8,128)S(1)} %get-tuple-element.36), channel_id=1, source_target_pairs={{1,0},{2,1},{3,2},{4,3},{5,4},{6,5},{7,6},{8,7},{9,8},{10,9},{11,1... | collective-permute-start | bytes 1572872 | tf_op jit(solution)/shard_map/ppermute | solution.py:22
  91.1 24.0 %collective-permute-start.6 = (f32[2,8,1,32,256]{4,3,2,1,0:T(8,128)S(1)}, f32[2,8,1,32,256]{4,3,2,1,0:T(8,128)S(1)}, u32[]{:S(2)}, u32[]{:S(2)}) collective-permute-start(f32[2,8,1,32,256]{4,3,2,1,0:T(8,128)S(1)} %get-tuple-element.33), channel_id=1, source_target_pairs={{0,1},{1,2},{2,3},{3,4},{4,5},{5,6},{6,7},{7,8},{8,9},{9,10},{10,1... | collective-permute-start | bytes 1572872 | tf_op jit(solution)/shard_map/ppermute | solution.py:20
  95.2 19.9 collective-permute-start.7
  120.1 22.0 %all-to-all-start.1 = ((f32[16,2,32,256]{3,1,0,2:T(2,128)}), f32[16,2,32,256]{3,1,0,2:T(2,128)S(1)}, u32[]{:S(2)}, u32[]{:S(2)}) async-start(f32[16,2,32,256]{3,1,0,2:T(2,128)} %copy.36), calls=%async_computation.1 | async-start | bytes 2097152 | tf_op jit(solution)/shard_map/all_to_all | solution.py:133
  127.0 1491.4 %all-gather.3.cloned.1.call-start = ((), (), s32[]{:S(2)}) async-start(), calls=%async_computation.3 | async-start | bytes 33619968 | tf_op jit(solution)/shard_map/all_gather | solution.py:102
  149.9 1752.9 %all-reduce.6.cloned.1.call-start = ((), (), s32[]{:S(2)}) async-start(), calls=%async_computation.2 | async-start | bytes 131072 | tf_op jit(solution)/shard_map/psum | solution.py:137
  1631.4 5.0 copy-start
  1908.6 111.0 %copy-start.1 = (f32[64,256]{1,0:T(8,128)S(1)}, f32[64,256]{1,0:T(8,128)}, u32[]{:S(2)}) copy-start(f32[64,256]{1,0:T(8,128)} %all-reduce.6.cloned.1.call-done) | copy-start | bytes 196612
Sparse Core Ops, SparseCore 0:
  150.0 1468.3 all-gather.2
  1641.1 261.6 all-reduce.5
